TPU v7x, 256 devices: a whole 4x4x8 slice. The times are simulated.
256 devices in a mesh: gx: 8 (over y, core), gy: 16 (over x_lo, z), src: 2 (over x_hi).
Axes of the slice: x: 4 (x_hi: 2, x_lo: 2; x = x_hi * 2 + x_lo), y: 4, z: 8, core: 2. Of those that a mesh axis runs over, the one named last changes fastest.
Arguments:
- conductivity: float32 [16, 128, 128], P('gx', 'gy'), may hold values from 0.3 to 3
- electrodes: int32 [128, 2], replicated, may hold values from 0 to 262143
- pair_order: int32 [128], P('src'), may hold values from 0 to 127, each once
- initial_fields: float32 [128, 16, 128, 128], P('src', 'gx', 'gy'), as said below
- adjoint_fields: float32 [128, 16, 128, 128], P('src', 'gx', 'gy'), may hold values from -6 to 6
Outputs:
- potentials: float32 [128, 16, 128, 128], P('src', 'gx', 'gy')
- gradient: float32 [16, 128, 128], P('gx', 'gy', 'src')
Inputs may be any that keep to these rules, and one draw needn't show every extreme that they name: `electrodes`: flat cell index (x * 128 + y) * 128 + z. `pair_order`: each pair appears once. `initial_fields`: every entry lies within 6 / sqrt(262144) in magnitude.
All inputs are finite; a program needn't handle non-finite values.
Results may differ from a plain program's by a relative error of at most 0.00029.
Values sent between devices are 32-bit elements; how exact they have to be, the bound alone decides.
No kernel may reach another device: no remote copies, remote signals or barrier semaphores. Data moves between devices by JAX's collectives and lax.ppermute only.
A program may use at most 64 MiB of HBM per device.

v0:
```python
import jax
import jax.numpy as jnp
from jax import lax
from jax.sharding import PartitionSpec as P

ITERS = 2
INJECT = 4.0


def padded_2(block, sides, width):
    for axis, dim in sides:
        count = lax.axis_size(axis)
        forward = [(i, i + 1) for i in range(count - 1)]
        backward = [(target, source) for source, target in forward]
        low = lax.ppermute(
            lax.slice_in_dim(block, block.shape[dim] - width, None, axis=dim), axis, forward
        )
        high = lax.ppermute(lax.slice_in_dim(block, 0, width, axis=dim), axis, backward)
        block = jnp.concatenate([low, block, high], axis=dim)
    return block


def conductances(sig_pad):
    full = jnp.pad(sig_pad, ((0, 0), (0, 0), (1, 1)))
    cond_x = 0.5 * (full[1:, 1:-1, 1:-1] + full[:-1, 1:-1, 1:-1])
    cond_y = 0.5 * (full[1:-1, 1:, 1:-1] + full[1:-1, :-1, 1:-1])
    cond_z = 0.5 * (full[1:-1, 1:-1, 1:] + full[1:-1, 1:-1, :-1])
    return (cond_x, cond_y, cond_z)


def operator(padded, conds):
    full = jnp.pad(padded, ((0, 0), (0, 0), (0, 0), (1, 1)))
    flux_x = conds[0] * (full[:, 1:, 1:-1, 1:-1] - full[:, :-1, 1:-1, 1:-1])
    flux_y = conds[1] * (full[:, 1:-1, 1:, 1:-1] - full[:, 1:-1, :-1, 1:-1])
    flux_z = conds[2] * (full[:, 1:-1, 1:-1, 1:] - full[:, 1:-1, 1:-1, :-1])
    return (
        flux_x[:, :-1]
        - flux_x[:, 1:]
        + (flux_y[:, :, :-1] - flux_y[:, :, 1:])
        + (flux_z[..., :-1] - flux_z[..., 1:])
    )


def gram_of(left, right):
    return jnp.einsum("axyz,bxyz->ab", left, right, precision=lax.Precision.HIGHEST)


def combine_cols(field, matrix):
    return jnp.einsum("axyz,ab->bxyz", field, matrix, precision=lax.Precision.HIGHEST)


def posdef_solve(matrix, right):
    lower = jnp.linalg.cholesky(matrix)
    middle = lax.linalg.triangular_solve(lower, right, left_side=True, lower=True)
    return lax.linalg.triangular_solve(lower, middle, left_side=True, lower=True, transpose_a=True)


def one_hot(cells, start, count):
    return (cells[:, None] == start + jnp.arange(count, dtype=jnp.int32)[None, :]).astype(
        jnp.float32
    )


def face_terms(field_pad, adjoint_pad):
    fu = jnp.pad(field_pad, ((0, 0), (0, 0), (0, 0), (1, 1)))
    fl = jnp.pad(adjoint_pad, ((0, 0), (0, 0), (0, 0), (1, 1)))
    term_x = jnp.sum(
        (fu[:, 1:, 1:-1, 1:-1] - fu[:, :-1, 1:-1, 1:-1])
        * (fl[:, 1:, 1:-1, 1:-1] - fl[:, :-1, 1:-1, 1:-1]),
        axis=0,
    )
    term_y = jnp.sum(
        (fu[:, 1:-1, 1:, 1:-1] - fu[:, 1:-1, :-1, 1:-1])
        * (fl[:, 1:-1, 1:, 1:-1] - fl[:, 1:-1, :-1, 1:-1]),
        axis=0,
    )
    term_z = jnp.sum(
        (fu[:, 1:-1, 1:-1, 1:] - fu[:, 1:-1, 1:-1, :-1])
        * (fl[:, 1:-1, 1:-1, 1:] - fl[:, 1:-1, 1:-1, :-1]),
        axis=0,
    )
    return (term_x, term_y, term_z)


def on_device(conductivity, electrodes, pair_order, initial_fields, adjoint_fields):
    cells_x, cells_y, cells_z = conductivity.shape
    columns = initial_fields.shape[0]
    total_y = lax.axis_size("gy") * cells_y
    start_x = lax.axis_index("gx") * cells_x
    start_y = lax.axis_index("gy") * cells_y
    picked = jnp.take(electrodes, pair_order, axis=0)

    def point_source(flat):
        xs = flat // (total_y * cells_z)
        ys = flat // cells_z % total_y
        zs = flat % cells_z
        return jnp.einsum(
            "cx,cy,cz->cxyz",
            one_hot(xs, start_x, cells_x),
            one_hot(ys, start_y, cells_y),
            one_hot(zs, 0, cells_z),
        )

    right = INJECT * (point_source(picked[:, 0]) - point_source(picked[:, 1]))
    stacked = jnp.concatenate([conductivity[None], initial_fields], axis=0)
    padded = padded_2(stacked, (("gx", 1), ("gy", 2)), 1)
    conds = conductances(padded[0])
    iterate = initial_fields
    iter_pad = padded[1:]
    residual = right - operator(iter_pad, conds)
    direction = residual
    res_gram = lax.psum(gram_of(residual, residual), ("gx", "gy"))
    for iteration in range(ITERS):
        dir_pad = padded_2(direction, (("gx", 1), ("gy", 2)), 1)
        image = operator(dir_pad, conds)
        curv_gram = lax.psum(gram_of(direction, image), ("gx", "gy"))
        step_mat = posdef_solve(curv_gram, res_gram)
        iterate = iterate + combine_cols(direction, step_mat)
        residual = residual - combine_cols(image, step_mat)
        if iteration + 1 < ITERS:
            new_gram = lax.psum(gram_of(residual, residual), ("gx", "gy"))
            turn_mat = posdef_solve(res_gram, new_gram)
            direction = residual + combine_cols(direction, turn_mat)
            res_gram = new_gram
    both = jnp.concatenate([iterate, adjoint_fields], axis=0)
    both_pad = padded_2(both, (("gx", 1), ("gy", 2)), 1)
    term_x, term_y, term_z = face_terms(both_pad[:columns], both_pad[columns:])
    local_grad = (
        -0.5
        / columns
        * (
            term_x[:-1]
            + term_x[1:]
            + term_y[:, :-1]
            + term_y[:, 1:]
            + term_z[..., :-1]
            + term_z[..., 1:]
        )
    )
    share = cells_z // lax.axis_size("src")
    summed = lax.psum(local_grad, "src")
    gradient = lax.dynamic_slice_in_dim(summed, lax.axis_index("src") * share, share, 2)
    return (iterate, gradient)


def solution(mesh):
    placed = (
        P("gx", "gy", None),
        P(),
        P("src"),
        P("src", "gx", "gy", None),
        P("src", "gx", "gy", None),
    )
    return jax.shard_map(
        on_device,
        mesh=mesh,
        in_specs=placed,
        out_specs=(P("src", "gx", "gy", None), P("gx", "gy", "src")),
        check_vma=False,
    )
```

profile of v0, /device:TPU:40, one launch (start us, length us, event | category | flops | bytes accessed | tf_op | source)
XLA Modules:
  0.0 1785.7 jit_solution(18146952785579994291)
XLA Ops:
  0.6 1.2 copy.47
  1.9 0.8 fusion.36
  2.6 1.9 collective-permute-start
  4.5 3.6 collective-permute-start.1
  9.5 0.8 copy.37
  11.6 0.8 collective-permute-done.1
  12.4 3.8 collective-permute-start.2
  16.3 2.0 collective-permute-start.3
  18.3 1.9 collective-permute-done.2
  20.2 3.9 collective-permute-done.3
  24.3 0.8 select_maximum_fusion.8
  26.2 1.9 collective-permute-start.4
  28.1 2.5 collective-permute-start.5
  32.0 3.8 collective-permute-done.5
  35.8 2.0 collective-permute-start.6
  37.9 4.8 collective-permute-start.7
  42.8 1.5 collective-permute-done.6
  44.3 1.2 collective-permute-done.7
  45.5 0.7 select_maximum_fusion.4
  47.5 485.9 %all-reduce.6 = (f32[64,64]{0,1:T(8,128)S(1)}, f32[64,64]{0,1:T(8,128)S(1)}) all-reduce(f32[64,64]{0,1:T(8,128)S(1)} %convolution_bitcast_fusion.5, f32[64,64]{0,1:T(8,128)S(1)} %convolution_bitcast_fusion.6), channel_id=1, replica_groups=mesh['gx'=8,'gy'=16,'src'=2] {'gx','gy'}, use_global_device_ids=true, to_apply=%region_3.5 | all-reduce | flops 8192 | bytes 65536 | tf_op jit(solution)/shard_map/psum | solution.py:112
  533.5 5.8 cholesky.70
  540.7 4.9 custom-call.15
  545.7 5.8 cholesky.59
  552.9 4.9 custom-call.13
  559.4 550.9 %psum.37 = f32[64,64]{1,0:T(8,128)S(1)} all-reduce(f32[64,64]{1,0:T(8,128)S(1)} %convolution_bitcast_fusion.3), channel_id=1, replica_groups=mesh['gx'=8,'gy'=16,'src'=2] {'gx','gy'}, use_global_device_ids=true, to_apply=%region_4.8 | all-reduce | flops 4096 | bytes 32768 | tf_op jit(solution)/shard_map/psum | solution.py:121
  1111.4 38.1 %collective-permute-start.8 = (f32[64,1,8,128]{3,0,2,1:T(8,128)S(1)}, f32[64,1,8,128]{3,0,2,1:T(8,128)S(1)}, u32[]{:S(2)}, u32[]{:S(2)}) collective-permute-start(f32[64,1,8,128]{3,0,2,1:T(8,128)S(1)} %get-tuple-element.39), channel_id=1, source_target_pairs={{32,0},{64,32},{96,64},{128,96},{160,128},{192,160},{224,192},{33,... | collective-permute-start | bytes 786440 | tf_op jit(solution)/shard_map/ppermute | solution.py:18
  1149.5 1.9 collective-permute-start.9
  1151.4 0.7 convolution_add_fusion.2
  1152.1 1.2 collective-permute-done.8
  1153.4 27.1 %collective-permute-done.9 = f32[64,1,8,128]{3,0,2,1:T(8,128)S(1)} collective-permute-done((f32[64,1,8,128]{3,0,2,1:T(8,128)S(1)}, f32[64,1,8,128]{3,0,2,1:T(8,128)S(1)}, u32[]{:S(2)}, u32[]{:S(2)}) %collective-permute-start.9) | collective-permute-done | bytes 262176 | tf_op jit(solution)/shard_map/ppermute | solution.py:15
  1180.5 5.1 collective-permute-start.10
  1185.6 1.9 collective-permute-start.11
  1188.1 4.4 collective-permute-done.11
  1192.5 0.7 select_maximum_fusion
  1193.7 0.7 convolution_bitcast_fusion.1
  1194.4 481.9 %psum.38 = f32[64,64]{0,1:T(8,128)S(1)} all-reduce(f32[64,64]{0,1:T(8,128)S(1)} %convolution_bitcast_fusion.1), channel_id=1, replica_groups=mesh['gx'=8,'gy'=16,'src'=2] {'gx','gy'}, use_global_device_ids=true, to_apply=%region_5.9 | all-reduce | flops 4096 | bytes 32768 | tf_op jit(solution)/shard_map/psum | solution.py:116
  1676.4 5.8 cholesky.81
  1683.6 4.9 custom-call.17
  1689.7 37.9 %collective-permute-start.12 = (f32[128,1,8,128]{3,0,2,1:T(8,128)S(1)}, f32[128,1,8,128]{3,0,2,1:T(8,128)S(1)}, u32[]{:S(2)}, u32[]{:S(2)}) collective-permute-start(f32[128,1,8,128]{3,0,2,1:T(8,128)S(1)} %get-tuple-element.31), channel_id=1, source_target_pairs={{32,0},{64,32},{96,64},{128,96},{160,128},{192,160},{224,192},{33,... | collective-permute-start | bytes 1572872 | tf_op jit(solution)/shard_map/ppermute | solution.py:18
  1727.5 1.9 collective-permute-start.13
  1729.5 1.1 copy.55
  1730.6 3.6 collective-permute-done.12
  1734.2 27.1 %collective-permute-done.13 = f32[128,1,8,128]{3,0,2,1:T(8,128)S(1)} collective-permute-done((f32[128,1,8,128]{3,0,2,1:T(8,128)S(1)}, f32[128,1,8,128]{3,0,2,1:T(8,128)S(1)}, u32[]{:S(2)}, u32[]{:S(2)}) %collective-permute-start.13) | collective-permute-done | bytes 524320 | tf_op jit(solution)/shard_map/ppermute | solution.py:15
  1761.4 7.5 collective-permute-start.14
  1768.8 1.9 collective-permute-start.15
  1771.5 1.2 collective-permute-done.14
  1772.7 4.4 collective-permute-done.15
  1778.6 6.5 psum.39
  (84 shorter events, 18.5 us)
Async XLA Ops:
  0.6 11.8 copy-start.2
  2.6 9.0 collective-permute-start
  4.5 7.9 collective-permute-start.1
  12.4 7.7 collective-permute-start.2
  16.3 7.8 collective-permute-start.3
  25.6 5.0 copy-start.1
  26.2 5.8 collective-permute-start.4
  28.1 7.7 collective-permute-start.5
  35.8 8.5 collective-permute-start.6
  37.9 7.6 collective-permute-start.7
  558.3 593.2 %copy-start = (f32[64,2,8,128]{3,2,1,0:T(8,128)S(1)}, f32[64,2,8,128]{3,2,1,0:T(8,128)}, u32[]{:S(2)}) copy-start(f32[64,2,8,128]{3,2,1,0:T(8,128)} %param.13) | copy-start | bytes 1572868
  1111.4 42.0 %collective-permute-start.8 = (f32[64,1,8,128]{3,0,2,1:T(8,128)S(1)}, f32[64,1,8,128]{3,0,2,1:T(8,128)S(1)}, u32[]{:S(2)}, u32[]{:S(2)}) collective-permute-start(f32[64,1,8,128]{3,0,2,1:T(8,128)S(1)} %get-tuple-element.39), channel_id=1, source_target_pairs={{32,0},{64,32},{96,64},{128,96},{160,128},{192,160},{224,192},{33,... | collective-permute-start | bytes 786440 | tf_op jit(solution)/shard_map/ppermute | solution.py:18
  1149.5 31.0 %collective-permute-start.9 = (f32[64,1,8,128]{3,0,2,1:T(8,128)S(1)}, f32[64,1,8,128]{3,0,2,1:T(8,128)S(1)}, u32[]{:S(2)}, u32[]{:S(2)}) collective-permute-start(f32[64,1,8,128]{3,0,2,1:T(8,128)S(1)} %get-tuple-element.38), channel_id=1, source_target_pairs={{0,32},{32,64},{64,96},{96,128},{128,160},{160,192},{192,224},{1,3... | collective-permute-start | bytes 786440 | tf_op jit(solution)/shard_map/ppermute | solution.py:15
  1180.5 7.6 collective-permute-start.10
  1185.6 6.9 collective-permute-start.11
  1689.7 44.6 %collective-permute-start.12 = (f32[128,1,8,128]{3,0,2,1:T(8,128)S(1)}, f32[128,1,8,128]{3,0,2,1:T(8,128)S(1)}, u32[]{:S(2)}, u32[]{:S(2)}) collective-permute-start(f32[128,1,8,128]{3,0,2,1:T(8,128)S(1)} %get-tuple-element.31), channel_id=1, source_target_pairs={{32,0},{64,32},{96,64},{128,96},{160,128},{192,160},{224,192},{33,... | collective-permute-start | bytes 1572872 | tf_op jit(solution)/shard_map/ppermute | solution.py:18
  1727.5 33.8 %collective-permute-start.13 = (f32[128,1,8,128]{3,0,2,1:T(8,128)S(1)}, f32[128,1,8,128]{3,0,2,1:T(8,128)S(1)}, u32[]{:S(2)}, u32[]{:S(2)}) collective-permute-start(f32[128,1,8,128]{3,0,2,1:T(8,128)S(1)} %get-tuple-element.30), channel_id=1, source_target_pairs={{0,32},{32,64},{64,96},{96,128},{128,160},{160,192},{192,224},{1,3... | collective-permute-start | bytes 1572872 | tf_op jit(solution)/shard_map/ppermute | solution.py:15
  1761.4 11.3 collective-permute-start.14
  1768.8 8.3 collective-permute-start.15
where the time goes:
time: 1790 us
  blocking collectives  1530 us (85%)
  starting transfers between devices  119 us (7%)
  waiting for transfers between devices  83.3 us (5%)
  other arithmetic  45.7 us (3%)
    psum x1, blocking collectives, on_device(): new_gram = lax.psum(gram_of(residual, residual), ('gx', 'gy'))  551 us
    psum x1, blocking collectives, on_device(): res_gram = lax.psum(gram_of(residual, residual), ('gx', 'gy'))  486 us
    psum x1, blocking collectives, on_device(): curv_gram = lax.psum(gram_of(direction, image), ('gx', 'gy'))  482 us
    ppermute x8, starting transfers between devices, padded_2(): lax.ppermute(lax.slice_in_dim(block, 0, width, axis=dim), axis, backward)  98.1 us
    ppermute x8, waiting for transfers between devices, padded_2(): lax.ppermute(lax.slice_in_dim(block, block.shape[dim] - width, None, axis...  69.9 us
  transfers between devices with their start and end apart: 16, of which 15 were waited for; matrix products, arithmetic and copies ran while one was open for 0% of the time, Pallas kernels for 0%

commit v1 on v0

--- a/solution.py
+++ b/solution.py
@@ -118,7 +118,7 @@
         iterate = iterate + combine_cols(direction, step_mat)
         residual = residual - combine_cols(image, step_mat)
         if iteration + 1 < ITERS:
-            new_gram = lax.psum(gram_of(residual, residual), ("gx", "gy"))
+            new_gram = jnp.sum(lax.all_gather(gram_of(residual, residual), ("gx", "gy")), axis=0)
             turn_mat = posdef_solve(res_gram, new_gram)
             direction = residual + combine_cols(direction, turn_mat)
             res_gram = new_gram

time: 1790 us -> 1600 us (0.89)
  blocking collectives: 1530 us -> 974 us
  waiting for transfers between devices: 83.3 us -> 453 us
  starting transfers between devices: 119 us -> 99.3 us
    psum x1 -> x0, blocking collectives: 551 us -> none  [on_device(): new_gram = lax.psum(gram_of(residual, residual), ('gx', 'gy'))]
    all_gather x0 -> x1, waiting for transfers between devices: none -> 395 us  [on_device(): lax.all_gather(gram_of(residual, residual), ('gx', 'gy'))]
    ppermute x8, waiting for transfers between devices: 69.9 us -> 43.7 us  [padded_2(): lax.ppermute(lax.slice_in_dim(block, block.shape[dim] - width, None, axis...]
    ppermute x8, starting transfers between devices: 98.1 us -> 75.1 us  [padded_2(): lax.ppermute(lax.slice_in_dim(block, 0, width, axis=dim), axis, backward)]
  transfers between devices with their start and end apart: 16 -> 17, of which waited for: 15 -> 16; matrix products, arithmetic and copies ran while one was open for 0% -> 1% of each run, Pallas kernels for 0% -> 0%
where the time goes in v1:
time: 1600 us
  blocking collectives  974 us (61%)
  waiting for transfers between devices  453 us (28%)
  starting transfers between devices  99.3 us (6%)
  other arithmetic  48.3 us (3%)
    psum x1, blocking collectives, on_device(): res_gram = lax.psum(gram_of(residual, residual), ('gx', 'gy'))  486 us
    psum x1, blocking collectives, on_device(): curv_gram = lax.psum(gram_of(direction, image), ('gx', 'gy'))  481 us
    all_gather x1, waiting for transfers between devices, on_device(): lax.all_gather(gram_of(residual, residual), ('gx', 'gy'))  395 us
    ppermute x8, starting transfers between devices, padded_2(): lax.ppermute(lax.slice_in_dim(block, 0, width, axis=dim), axis, backward)  75.1 us
    ppermute x8, waiting for transfers between devices, padded_2(): lax.ppermute(lax.slice_in_dim(block, block.shape[dim] - width, None, axis...  43.7 us
  transfers between devices with their start and end apart: 17, of which 16 were waited for; matrix products, arithmetic and copies ran while one was open for 1% of the time, Pallas kernels for 0%

profile of v1, /device:TPU:40, one launch (start us, length us, event | category | flops | bytes accessed | tf_op | source)
XLA Modules:
  0.0 1601.0 jit_solution(7764617981133681311)
XLA Ops:
  7.2 1.2 copy.47
  8.4 0.8 fusion.36
  9.2 1.9 collective-permute-start
  11.1 3.6 collective-permute-start.1
  16.1 0.8 copy.37
  18.2 0.8 collective-permute-done.1
  19.0 3.8 collective-permute-start.2
  22.9 2.0 collective-permute-start.3
  24.9 1.9 collective-permute-done.2
  26.8 3.9 collective-permute-done.3
  30.9 0.8 select_maximum_fusion.8
  32.8 1.9 collective-permute-start.4
  34.7 2.5 collective-permute-start.5
  37.8 0.8 collective-permute-done.4
  38.6 3.8 collective-permute-done.5
  42.4 2.0 collective-permute-start.6
  44.4 4.8 collective-permute-start.7
  49.4 1.5 collective-permute-done.6
  50.9 1.2 collective-permute-done.7
  54.1 486.1 %all-reduce.6 = (f32[64,64]{0,1:T(8,128)S(1)}, f32[64,64]{0,1:T(8,128)S(1)}) all-reduce(f32[64,64]{0,1:T(8,128)S(1)} %convolution_bitcast_fusion.5, f32[64,64]{0,1:T(8,128)S(1)} %convolution_bitcast_fusion.6), channel_id=1, replica_groups=mesh['gx'=8,'gy'=16,'src'=2] {'gx','gy'}, use_global_device_ids=true, to_apply=%region_3.5 | all-reduce | flops 8192 | bytes 65536 | tf_op jit(solution)/shard_map/psum | solution.py:112
  540.2 5.8 cholesky.59
  547.4 4.9 custom-call.13
  553.4 1.2 convolution_bitcast_fusion.3
  554.9 5.8 cholesky.70
  562.1 4.9 custom-call.15
  567.0 395.3 %all-gather.3.cloned.1.call-done = f32[8192,64]{1,0:T(8,128)} async-done(((f32[64,64]{1,0:T(8,128)}), f32[8192,64]{1,0:T(8,128)}) %all-gather.3.cloned.1.call-update) | async-done | bytes 2097168 | tf_op jit(solution)/shard_map/all_gather | solution.py:121
  962.2 2.6 reduce_sum.36
  965.9 18.6 %collective-permute-start.8 = (f32[64,1,8,128]{3,0,2,1:T(8,128)S(1)}, f32[64,1,8,128]{3,0,2,1:T(8,128)S(1)}, u32[]{:S(2)}, u32[]{:S(2)}) collective-permute-start(f32[64,1,8,128]{3,0,2,1:T(8,128)S(1)} %get-tuple-element.39), channel_id=1, source_target_pairs={{32,0},{64,32},{96,64},{128,96},{160,128},{192,160},{224,192},{33,... | collective-permute-start | bytes 786440 | tf_op jit(solution)/shard_map/ppermute | solution.py:18
  984.6 1.9 collective-permute-start.9
  987.2 1.2 collective-permute-done.8
  988.5 3.8 collective-permute-done.9
  992.3 1.9 collective-permute-start.10
  994.2 5.4 collective-permute-start.11
  999.7 0.9 collective-permute-done.10
  1000.6 1.5 collective-permute-done.11
  1004.0 481.1 %psum.30 = f32[64,64]{0,1:T(8,128)S(1)} all-reduce(f32[64,64]{0,1:T(8,128)S(1)} %convolution_bitcast_fusion.1), channel_id=1, replica_groups=mesh['gx'=8,'gy'=16,'src'=2] {'gx','gy'}, use_global_device_ids=true, to_apply=%region_5.9 | all-reduce | flops 4096 | bytes 32768 | tf_op jit(solution)/shard_map/psum | solution.py:116
  1485.2 5.8 cholesky.81
  1492.4 4.9 custom-call.17
  1498.5 37.9 %collective-permute-start.12 = (f32[128,1,8,128]{3,0,2,1:T(8,128)S(1)}, f32[128,1,8,128]{3,0,2,1:T(8,128)S(1)}, u32[]{:S(2)}, u32[]{:S(2)}) collective-permute-start(f32[128,1,8,128]{3,0,2,1:T(8,128)S(1)} %get-tuple-element.31), channel_id=1, source_target_pairs={{32,0},{64,32},{96,64},{128,96},{160,128},{192,160},{224,192},{33,... | collective-permute-start | bytes 1572872 | tf_op jit(solution)/shard_map/ppermute | solution.py:18
  1536.4 1.9 collective-permute-start.13
  1538.3 1.1 copy.55
  1539.4 3.6 collective-permute-done.12
  1543.1 27.1 %collective-permute-done.13 = f32[128,1,8,128]{3,0,2,1:T(8,128)S(1)} collective-permute-done((f32[128,1,8,128]{3,0,2,1:T(8,128)S(1)}, f32[128,1,8,128]{3,0,2,1:T(8,128)S(1)}, u32[]{:S(2)}, u32[]{:S(2)}) %collective-permute-start.13) | collective-permute-done | bytes 524320 | tf_op jit(solution)/shard_map/ppermute | solution.py:15
  1570.2 7.0 collective-permute-start.14
  1577.2 1.9 collective-permute-start.15
  1579.9 1.2 collective-permute-done.14
  1581.1 4.4 collective-permute-done.15
  1587.0 6.5 psum.31
  (87 shorter events, 19.8 us)
Async XLA Ops:
  7.2 11.8 copy-start.2
  7.2 955.1 %all-gather.3.cloned.1.call-start = ((), (), s32[]{:S(2)}) async-start(), calls=%async_computation | async-start | bytes 4227072 | tf_op jit(solution)/shard_map/all_gather | solution.py:121
  9.2 9.0 collective-permute-start
  11.1 7.9 collective-permute-start.1
  19.0 7.7 collective-permute-start.2
  22.9 7.8 collective-permute-start.3
  32.8 5.8 collective-permute-start.4
  34.7 7.7 collective-permute-start.5
  42.4 8.5 collective-permute-start.6
  44.4 7.6 collective-permute-start.7
  53.5 501.1 %copy-start.1 = (f32[64,2,8,128]{3,2,1,0:T(8,128)S(1)}, f32[64,2,8,128]{3,2,1,0:T(8,128)}, u32[]{:S(2)}) copy-start(f32[64,2,8,128]{3,2,1,0:T(8,128)} %param.14) | copy-start | bytes 1572868
  962.2 24.3 %copy-start = (f32[64,2,8,128]{3,2,1,0:T(8,128)S(1)}, f32[64,2,8,128]{3,2,1,0:T(8,128)}, u32[]{:S(2)}) copy-start(f32[64,2,8,128]{3,2,1,0:T(8,128)} %param.13) | copy-start | bytes 1572868
  965.9 22.5 %collective-permute-start.8 = (f32[64,1,8,128]{3,0,2,1:T(8,128)S(1)}, f32[64,1,8,128]{3,0,2,1:T(8,128)S(1)}, u32[]{:S(2)}, u32[]{:S(2)}) collective-permute-start(f32[64,1,8,128]{3,0,2,1:T(8,128)S(1)} %get-tuple-element.39), channel_id=1, source_target_pairs={{32,0},{64,32},{96,64},{128,96},{160,128},{192,160},{224,192},{33,... | collective-permute-start | bytes 786440 | tf_op jit(solution)/shard_map/ppermute | solution.py:18
  984.6 7.7 collective-permute-start.9
  992.3 8.3 collective-permute-start.10
  994.2 7.9 collective-permute-start.11
  1498.5 44.5 %collective-permute-start.12 = (f32[128,1,8,128]{3,0,2,1:T(8,128)S(1)}, f32[128,1,8,128]{3,0,2,1:T(8,128)S(1)}, u32[]{:S(2)}, u32[]{:S(2)}) collective-permute-start(f32[128,1,8,128]{3,0,2,1:T(8,128)S(1)} %get-tuple-element.31), channel_id=1, source_target_pairs={{32,0},{64,32},{96,64},{128,96},{160,128},{192,160},{224,192},{33,... | collective-permute-start | bytes 1572872 | tf_op jit(solution)/shard_map/ppermute | solution.py:18
  1536.4 33.8 %collective-permute-start.13 = (f32[128,1,8,128]{3,0,2,1:T(8,128)S(1)}, f32[128,1,8,128]{3,0,2,1:T(8,128)S(1)}, u32[]{:S(2)}, u32[]{:S(2)}) collective-permute-start(f32[128,1,8,128]{3,0,2,1:T(8,128)S(1)} %get-tuple-element.30), channel_id=1, source_target_pairs={{0,32},{32,64},{64,96},{96,128},{128,160},{160,192},{192,224},{1,3... | collective-permute-start | bytes 1572872 | tf_op jit(solution)/shard_map/ppermute | solution.py:15
  1570.2 10.9 collective-permute-start.14
  1577.2 8.3 collective-permute-start.15
Sparse Core Ops, SparseCore 0:
  554.7 407.4 all-gather.2
